TPU v7x, 256 devices: a whole 4x4x8 slice. The times are simulated.
256 devices in a mesh: feat: 32 (over y, x, core), samp: 8 (over z).
Axes of the slice: x: 4, y: 4, z: 8, core: 2. Of those that a mesh axis runs over, the one named last changes fastest.
Arguments:
- hash_codes: int32 [32, 6144, 1024], P('feat', 'samp'), may hold values from 0 to 4095
- sample_index: int32 [32, 65536], P('feat', 'samp'), may hold values from 0 to 767, as said below
- labels: int32 [8192, 8], P('feat', 'samp'), may hold values 0 or 1
- encoder_first: bfloat16 [32, 1024, 2048], P('feat'), may hold values from -0.1875 to 0.1875
- encoder_second: bfloat16 [32, 2048, 256], P('feat'), may hold values from -0.125 to 0.125
- top_weight: bfloat16 [1024, 1024], replicated, may hold values from -0.1875 to 0.1875
- score_vector: bfloat16 [1024], replicated, may hold values from -0.1875 to 0.1875
Outputs:
- row_grads: float32 [32, 6144, 256], P('feat', 'samp')
- grad_first: float32 [32, 1024, 2048], P('feat', 'samp')
- grad_second: float32 [32, 2048, 256], P('feat', 'samp')
Inputs may be any that keep to these rules, and one draw needn't show every extreme that they name: `sample_index`: for each feature and sample group the slots used by the group's 8192 samples are 0 to some count minus 1, each at least once; for some feature and group that count is 768.
All inputs are finite; a program needn't handle non-finite values. No bound on the sum of `labels` on one device may be relied on, other than what follows from the above.
Results may differ from a plain program's by a relative error of at most 0.019.
Values may be sent and summed in bfloat16 or wider, within the bound.
No kernel may reach another device: no remote copies, remote signals or barrier semaphores. Data moves between devices by JAX's collectives and lax.ppermute only.
A program may use at most 128 MiB of HBM per device.

v0:
```python
import jax
import jax.numpy as jnp
from jax import lax
from jax.sharding import PartitionSpec as P

BUCKETS = 4096


loss_scale = 256.0


def silu_slope(inputs):
    logistic = jax.nn.sigmoid(inputs)
    return logistic * (1.0 + inputs * (1.0 - logistic))


def top_tower(picked, label_block, top_weight, score_vector):
    feats, count, width = picked.shape
    pair_dots = (
        jnp.einsum("fne,hne->nfh", picked, picked, preferred_element_type=jnp.float32)
        * width ** (-0.5)
    ).astype(jnp.bfloat16)
    pair_flat = pair_dots.reshape(count, feats * feats)
    top_pre = jnp.dot(pair_flat, top_weight, preferred_element_type=jnp.float32)
    top_hidden = jax.nn.silu(top_pre).astype(jnp.bfloat16)
    logits = jnp.dot(top_hidden, score_vector, preferred_element_type=jnp.float32)
    dlogit = loss_scale * (jax.nn.sigmoid(logits) - label_block.astype(jnp.float32))
    top_delta = (
        dlogit[:, None] * score_vector.astype(jnp.float32)[None, :] * silu_slope(top_pre)
    ).astype(jnp.bfloat16)
    pair_delta = jnp.einsum(
        "nk,jk->nj", top_delta, top_weight, preferred_element_type=jnp.float32
    ).reshape(count, feats, feats)
    pair_sym = (pair_delta + jnp.swapaxes(pair_delta, 1, 2)).astype(jnp.bfloat16)
    emb_delta = jnp.einsum(
        "nfh,hne->fne", pair_sym, picked, preferred_element_type=jnp.float32
    ) * width ** (-0.5)
    return emb_delta.astype(jnp.bfloat16)


def local(
    hash_codes, sample_index, labels, encoder_first, encoder_second, top_weight, score_vector
):
    feat_count = lax.axis_size("feat")
    encoded = (hash_codes[0].astype(jnp.float32) * (2.0 / (BUCKETS - 1)) - 1.0).astype(jnp.bfloat16)
    first_pre = jnp.dot(encoded, encoder_first[0], preferred_element_type=jnp.float32)
    first_hidden = jax.nn.silu(first_pre).astype(jnp.bfloat16)
    row_table = jnp.dot(first_hidden, encoder_second[0], preferred_element_type=jnp.float32).astype(
        jnp.bfloat16
    )
    positions = sample_index[0]
    slot_count = row_table.shape[0]
    emb_width = row_table.shape[1]
    chosen_rows = jnp.take(row_table, positions, axis=0).reshape(feat_count, -1, emb_width)
    picked = lax.all_to_all(chosen_rows, "feat", split_axis=0, concat_axis=0, tiled=True)
    emb_delta = top_tower(picked, labels[:, 0], top_weight, score_vector)
    returned = lax.all_to_all(emb_delta, "feat", split_axis=0, concat_axis=0, tiled=True)
    row_grads = jax.ops.segment_sum(
        returned.reshape(-1, emb_width).astype(jnp.float32), positions, num_segments=slot_count
    )
    row_delta = row_grads.astype(jnp.bfloat16)
    second_local = jnp.einsum(
        "rk,re->ke", first_hidden, row_delta, preferred_element_type=jnp.float32
    )
    first_back = jnp.einsum(
        "re,ke->rk", row_delta, encoder_second[0], preferred_element_type=jnp.float32
    )
    first_delta = (first_back * silu_slope(first_pre)).astype(jnp.bfloat16)
    first_local = jnp.einsum("rh,rk->hk", encoded, first_delta, preferred_element_type=jnp.float32)
    total_first, total_second = (
        lax.psum(first_local.astype(jnp.bfloat16), "samp").astype(jnp.float32),
        lax.psum(second_local.astype(jnp.bfloat16), "samp").astype(jnp.float32),
    )
    shard_id = lax.axis_index("samp")
    group_count = lax.axis_size("samp")
    first_rows = total_first.shape[0] // group_count
    second_rows = total_second.shape[0] // group_count
    share_first = lax.dynamic_slice_in_dim(total_first, shard_id * first_rows, first_rows, 0)
    share_second = lax.dynamic_slice_in_dim(total_second, shard_id * second_rows, second_rows, 0)
    return (row_grads[None], share_first[None], share_second[None])


def solution(mesh):
    return jax.shard_map(
        local,
        mesh=mesh,
        in_specs=(
            P("feat", "samp", None),
            P("feat", "samp"),
            P("feat", "samp"),
            P("feat", None, None),
            P("feat", None, None),
            P(),
            P(),
        ),
        out_specs=(P("feat", "samp", None), P("feat", "samp", None), P("feat", "samp", None)),
        check_vma=False,
    )
```

profile of v0, /device:TPU:1, one launch (start us, length us, event | category | flops | bytes accessed | tf_op | source)
XLA Modules:
  0.0 400.1 jit_solution(6173155816172626765)
XLA Ops:
  7.2 0.0 copy-start
  7.2 0.9 compare_select_fusion
  8.1 0.5 broadcast.66
  8.7 1.5 reduce.3
  10.2 0.0 copy-start.5
  10.2 9.8 %multiply_convert_fusion.2 = (bf16[768,2048]{1,0:T(8,128)(2,1)S(1)}, f32[768,2048]{1,0:T(8,128)}) fusion(bf16[1,1024,2048]{2,1,0:T(8,128)(2,1)} %param.10, s32[1,768,1024]{2,1,0:T(8,128)} %param.7), kind=kOutput, calls=%fused_computation.6 | convolution fusion | flops 3232235520 | bytes 16777216 | tf_op jit(solution)/shard_map/dot_general | solution.py:46
  20.0 0.0 copy-start.6
  20.0 1.6 copy-done.6
  21.7 0.0 copy-done.5
  21.7 1.0 convolution_convert_fusion.2
  22.7 33.1 %gather_fusion = bf16[8192,256]{1,0:T(8,128)(2,1)} fusion(bf16[768,256]{1,0:T(8,128)(2,1)S(1)} %convolution_convert_fusion.2, s32[8192]{0:T(1024)S(1)} %broadcast_clamp_fusion), kind=kCustom, calls=%fused_computation | custom fusion | bytes 8421376 | tf_op jit(solution)/shard_map/jit(_take)/gather | solution.py:54
  55.7 5.2 %broadcast_select_fusion = bf16[32,256,256]{2,1,0:T(8,128)(2,1)} fusion(bf16[32,256,256]{2,1,0:T(8,128)(2,1)} %bitcast.47, pred[32,256]{1,0:T(8,128)(4,1)S(1)} %compare_and_fusion), kind=kLoop, calls=%fused_computation.11 | loop fusion | flops 2097152 | bytes 8396800 | tf_op jit(solution)/shard_map/jit(_take)/select_n | solution.py:54
  61.0 0.0 copy-start.3
  61.0 0.0 copy-start.4
  61.0 8.8 %all-to-all-start = ((bf16[32,256,256]{2,1,0:T(8,128)(2,1)}), bf16[32,256,256]{2,1,0:T(8,128)(2,1)}, u32[]{:S(2)}, u32[]{:S(2)}) async-start(bf16[32,256,256]{2,1,0:T(8,128)(2,1)} %broadcast_select_fusion), calls=%async_computation | async-start | bytes 8388608 | tf_op jit(solution)/shard_map/all_to_all | solution.py:55
  69.8 0.0 all-reduce.3.cloned.1.call-start
  69.8 0.0 copy-done.3
  69.9 0.0 copy-done.4
  69.9 50.2 %all-to-all-done = bf16[32,256,256]{2,1,0:T(8,128)(2,1)} async-done(((bf16[32,256,256]{2,1,0:T(8,128)(2,1)}), bf16[32,256,256]{2,1,0:T(8,128)(2,1)}, u32[]{:S(2)}, u32[]{:S(2)}) %all-to-all-start) | async-done | bytes 4194336 | tf_op jit(solution)/shard_map/all_to_all | solution.py:55
  120.0 10.2 %fusion.5 = f32[256,32,32]{2,1,0:T(8,128)} fusion(bf16[32,256,256]{2,1,0:T(8,128)(2,1)} %all-to-all-done), kind=kOutput, calls=%fused_computation.13 | convolution fusion | flops 134217728 | bytes 5242880 | tf_op jit(solution)/shard_map/fne,hne->nfh/dot_general | solution.py:20
  130.2 3.5 copy.33
  133.8 0.1 multiply_convert_fusion.5
  133.9 0.0 copy-done
  133.9 0.7 fusion.35
  134.6 0.4 fusion.20
  135.0 1.0 fusion.16
  136.0 0.6 fusion.12
  136.6 3.0 copy.37
  139.7 4.9 %fusion.2 = bf16[32,256,256]{2,0,1:T(8,128)(2,1)S(1)} fusion(bf16[256,32,32]{2,1,0:T(8,128)(2,1)S(1)} %copy.37, bf16[32,256,256]{2,1,0:T(8,128)(2,1)} %all-to-all-done), kind=kOutput, calls=%fused_computation.8 | convolution fusion | flops 138412032 | bytes 8912896 | tf_op jit(solution)/shard_map/nfh,hne->fne/dot_general | solution.py:35
  144.6 2.4 copy.38
  147.0 57.9 %all_to_all.10 = bf16[32,256,256]{2,1,0:T(8,128)(2,1)} all-to-all(bf16[32,256,256]{2,1,0:T(8,128)(2,1)S(1)} %copy.38), channel_id=1, replica_groups=mesh['feat'=32,'samp'=8] {'feat'}, dimensions={0} | all-to-all | bytes 8388608 | tf_op jit(solution)/shard_map/all_to_all | solution.py:57
  204.9 40.9 %scatter_custom_fusion = f32[768,256]{1,0:T(8,128)S(1)} fusion(s32[8192]{0:T(1024)} %bitcast.51, bf16[8192,256]{1,0:T(8,128)(2,1)} %bitcast.46, f32[]{:T(128)} %constant.15.clone.1), kind=kCustom, calls=%fused_computation.2 | custom fusion | flops 4194304 | bytes 4981248 | tf_op jit(solution)/shard_map/scatter-add | solution.py:58
  245.9 0.0 copy-start.2
  245.9 4.2 %convolution_convert_fusion.1 = bf16[2048,256]{1,0:T(8,128)(2,1)} fusion(bf16[768,2048]{1,0:T(8,128)(2,1)} %copy-done.6, f32[768,256]{1,0:T(8,128)S(1)} %scatter_custom_fusion), kind=kOutput, calls=%fused_computation.18 | convolution fusion | flops 806027264 | bytes 4980736 | tf_op jit(solution)/shard_map/rk,re->ke/dot_general | solution.py:62
  250.1 0.0 copy-done.2
  250.1 0.0 copy-start.1
  250.1 10.4 %convolution_convert_fusion = bf16[1024,2048]{1,0:T(8,128)(2,1)} fusion(f32[768,2048]{1,0:T(8,128)} %get-tuple-element.6, bf16[1,2048,256]{2,1,0:T(8,128)(2,1)} %param.11, s32[1,768,1024]{2,1,0:T(8,128)} %param.7, f32[768,256]{1,0:T(8,128)S(1)} %scatter_custom_fusion), kind=kOutput, calls=%fused_computation.12 | convolution fusion | flops 4046127104 | bytes 15466496 | tf_op jit(solution)/shard_map/rh,rk->hk/dot_general | solution.py:69
  260.5 0.0 all-reduce.3.cloned.1.call-update
  260.5 129.0 %all-reduce.3.cloned.1.call-done = (bf16[1024,2048]{1,0:T(8,128)(2,1)}, bf16[2048,256]{1,0:T(8,128)(2,1)}) async-done(((bf16[1024,2048]{1,0:T(8,128)(2,1)}, bf16[2048,256]{1,0:T(8,128)(2,1)}), (bf16[1024,2048]{1,0:T(8,128)(2,1)}, bf16[2048,256]{1,0:T(8,128)(2,1)})) %all-reduce.3.cloned.1.call-update) | async-done | bytes 5242896 | tf_op jit(solution)/shard_map/psum | solution.py:71
  389.5 2.1 convert_bitcast_fusion
  391.6 1.6 convert_bitcast_fusion.1
  393.2 0.0 copy-done.1
  (7 shorter events, 0.1 us)
Async XLA Ops:
  7.2 126.7 %copy-start = (bf16[1024,1024]{1,0:T(8,128)(2,1)S(1)}, bf16[1024,1024]{1,0:T(8,128)(2,1)}, u32[]{:S(2)}) copy-start(bf16[1024,1024]{1,0:T(8,128)(2,1)} %param.12) | copy-start | bytes 6291460
  10.2 11.5 %copy-start.5 = (bf16[1,2048,256]{2,1,0:T(8,128)(2,1)S(1)}, bf16[1,2048,256]{2,1,0:T(8,128)(2,1)}, u32[]{:S(2)}) copy-start(bf16[1,2048,256]{2,1,0:T(8,128)(2,1)} %param.11) | copy-start | bytes 3145732
  20.0 1.6 copy-start.6
  61.0 8.8 %copy-start.3 = (bf16[1024]{0:T(1024)(128)(2,1)S(1)}, bf16[1024]{0:T(1024)(128)(2,1)}, u32[]{:S(2)}) copy-start(bf16[1024]{0:T(1024)(128)(2,1)} %param.13) | copy-start | bytes 6148
  61.0 8.9 %copy-start.4 = (s32[256,1]{0,1:T(1,128)S(1)}, s32[256,1]{0,1:T(1,128)}, u32[]{:S(2)}) copy-start(s32[256,1]{0,1:T(1,128)} %param.9) | copy-start | bytes 3076
  61.0 59.0 %all-to-all-start = ((bf16[32,256,256]{2,1,0:T(8,128)(2,1)}), bf16[32,256,256]{2,1,0:T(8,128)(2,1)}, u32[]{:S(2)}, u32[]{:S(2)}) async-start(bf16[32,256,256]{2,1,0:T(8,128)(2,1)} %broadcast_select_fusion), calls=%async_computation | async-start | bytes 8388608 | tf_op jit(solution)/shard_map/all_to_all | solution.py:55
  69.8 319.7 %all-reduce.3.cloned.1.call-start = ((), (), s32[]{:S(2)}) async-start(), calls=%async_computation.2 | async-start | bytes 10485760 | tf_op jit(solution)/shard_map/psum | solution.py:71
  245.9 4.2 %copy-start.2 = (f32[768,256]{1,0:T(8,128)}, f32[768,256]{1,0:T(8,128)S(1)}, u32[]{:S(2)}) copy-start(f32[768,256]{1,0:T(8,128)S(1)} %scatter_custom_fusion) | copy-start | bytes 2359300
  250.1 143.2 %copy-start.1 = (bf16[1024,1024]{1,0:T(8,128)(2,1)S(1)}, bf16[1024,1024]{1,0:T(8,128)(2,1)}, u32[]{:S(2)}) copy-start(bf16[1024,1024]{1,0:T(8,128)(2,1)} %param.12) | copy-start | bytes 6291460
Sparse Core Ops, SparseCore 0:
  260.6 128.8 all-reduce.2
where the time goes:
time: 401 us; the launch traced here: 400 us
  waiting for transfers between devices  179 us (45%)
  blocking collectives  57.9 us (14%)
  other arithmetic  53.1 us (13%)
  local copies, waits for them, and re-layouts  44.2 us (11%)
  matrix products  42.7 us (11%)
  between operations  14.2 us (4%)
  starting transfers between devices  8.82 us (2%)
    psum x1, waiting for transfers between devices, local(): lax.psum(first_local.astype(jnp.bfloat16), 'samp').astype(jnp.float32)  129 us
    all_to_all x1, blocking collectives, local(): lax.all_to_all(emb_delta, 'feat', split_axis=0, concat_axis=0, tiled=True)  57.9 us
    all_to_all x1, waiting for transfers between devices, local(): lax.all_to_all(chosen_rows, 'feat', split_axis=0, concat_axis=0, tiled=True)  50.2 us
    scatter-add x1, other arithmetic, local(): jax.ops.segment_sum(returned.reshape(-1, emb_width).astype(jnp.float32),...  40.9 us
    gather x1, local copies, waits for them, and re-layouts, local(): jnp.take(row_table, positions, axis=0).reshape(feat_count, -1, emb_width)  33.1 us
    dot_general x1, matrix products, local(): jnp.einsum('rh,rk->hk', encoded, first_delta, preferred_element_type=jnp....  10.4 us
    dot_general x1, matrix products, top_tower(): jnp.einsum('fne,hne->nfh', picked, picked, preferred_element_type=jnp.flo...  10.2 us
    dot_general x1, matrix products, local(): jnp.dot(encoded, encoder_first[0], preferred_element_type=jnp.float32)  9.85 us
  transfers between devices with their start and end apart: 2, of which 2 were waited for; matrix products, arithmetic and copies ran while one was open for 0% of the time, Pallas kernels for 0%

commit v1 on v0

--- a/solution.py
+++ b/solution.py
@@ -51,12 +51,19 @@
     positions = sample_index[0]
     slot_count = row_table.shape[0]
     emb_width = row_table.shape[1]
-    chosen_rows = jnp.take(row_table, positions, axis=0).reshape(feat_count, -1, emb_width)
+    select = (positions[:, None] == lax.broadcasted_iota(jnp.int32, (1, slot_count), 1)).astype(
+        jnp.bfloat16
+    )
+    chosen_rows = (
+        jnp.dot(select, row_table, preferred_element_type=jnp.float32)
+        .astype(jnp.bfloat16)
+        .reshape(feat_count, -1, emb_width)
+    )
     picked = lax.all_to_all(chosen_rows, "feat", split_axis=0, concat_axis=0, tiled=True)
     emb_delta = top_tower(picked, labels[:, 0], top_weight, score_vector)
     returned = lax.all_to_all(emb_delta, "feat", split_axis=0, concat_axis=0, tiled=True)
-    row_grads = jax.ops.segment_sum(
-        returned.reshape(-1, emb_width).astype(jnp.float32), positions, num_segments=slot_count
+    row_grads = jnp.einsum(
+        "nu,ne->ue", select, returned.reshape(-1, emb_width), preferred_element_type=jnp.float32
     )
     row_delta = row_grads.astype(jnp.bfloat16)
     second_local = jnp.einsum(
@@ -67,16 +74,12 @@
     )
     first_delta = (first_back * silu_slope(first_pre)).astype(jnp.bfloat16)
     first_local = jnp.einsum("rh,rk->hk", encoded, first_delta, preferred_element_type=jnp.float32)
-    total_first, total_second = (
-        lax.psum(first_local.astype(jnp.bfloat16), "samp").astype(jnp.float32),
-        lax.psum(second_local.astype(jnp.bfloat16), "samp").astype(jnp.float32),
-    )
-    shard_id = lax.axis_index("samp")
-    group_count = lax.axis_size("samp")
-    first_rows = total_first.shape[0] // group_count
-    second_rows = total_second.shape[0] // group_count
-    share_first = lax.dynamic_slice_in_dim(total_first, shard_id * first_rows, first_rows, 0)
-    share_second = lax.dynamic_slice_in_dim(total_second, shard_id * second_rows, second_rows, 0)
+    share_first = lax.psum_scatter(
+        first_local.astype(jnp.bfloat16), "samp", scatter_dimension=0, tiled=True
+    ).astype(jnp.float32)
+    share_second = lax.psum_scatter(
+        second_local.astype(jnp.bfloat16), "samp", scatter_dimension=0, tiled=True
+    ).astype(jnp.float32)
     return (row_grads[None], share_first[None], share_second[None])
 
 

time: 401 us -> 300 us (0.75)
  other arithmetic: 53.1 us -> 4.47 us
  waiting for transfers between devices: 179 us -> 133 us
  local copies, waits for them, and re-layouts: 44.2 us -> 10.6 us
  matrix products: 42.7 us -> 59.5 us
  blocking collectives: 57.9 us -> 65.6 us
    psum x1 -> x0, waiting for transfers between devices: 129 us -> none  [local(): lax.psum(first_local.astype(jnp.bfloat16), 'samp').astype(jnp.float32)]
    reduce_scatter x0 -> x2, waiting for transfers between devices: none -> 82.8 us  [the longest x1 60 us: local(): lax.psum_scatter(first_local.astype(jnp.bfloat16), 'samp', scatter_dimens...]
    scatter-add x1 -> x0, other arithmetic: 40.9 us -> none  [local(): jax.ops.segment_sum(returned.reshape(-1, emb_width).astype(jnp.float32),...]
    gather x1 -> x0, local copies, waits for them, and re-layouts: 33.1 us -> none  [local(): jnp.take(row_table, positions, axis=0).reshape(feat_count, -1, emb_width)]
    dot_general x1 -> x2, matrix products: 0.98 us -> 18.4 us  [the longest x1 10.5 us: local(): jnp.dot(select, row_table, preferred_element_type=jnp.float32)]
    all_to_all x1, blocking collectives: 57.9 us -> 65.6 us  [local(): lax.all_to_all(emb_delta, 'feat', split_axis=0, concat_axis=0, tiled=True)]
    select_n x2 -> x0, other arithmetic: 6.19 us -> none  [local(): jnp.take(row_table, positions, axis=0).reshape(feat_count, -1, emb_width)]
  transfers between devices with their start and end apart: 2 -> 3, of which waited for: 2 -> 3; matrix products, arithmetic and copies ran while one was open for 0% -> 4% of each run, Pallas kernels for 0% -> 0%
where the time goes in v1:
time: 300 us; the launch traced here: 296 us
  waiting for transfers between devices  133 us (44%)
  blocking collectives  65.6 us (22%)
  matrix products  59.5 us (20%)
  between operations  14.4 us (5%)
  local copies, waits for them, and re-layouts  10.6 us (4%)
  starting transfers between devices  9.12 us (3%)
  other arithmetic  4.47 us (1%)
    all_to_all x1, blocking collectives, local(): lax.all_to_all(emb_delta, 'feat', split_axis=0, concat_axis=0, tiled=True)  65.6 us
    reduce_scatter x1, waiting for transfers between devices, local(): lax.psum_scatter(first_local.astype(jnp.bfloat16), 'samp', scatter_dimens...  60 us
    all_to_all x1, waiting for transfers between devices, local(): lax.all_to_all(chosen_rows, 'feat', split_axis=0, concat_axis=0, tiled=True)  49.9 us
    reduce_scatter x1, waiting for transfers between devices, local(): lax.psum_scatter(second_local.astype(jnp.bfloat16), 'samp', scatter_dimen...  22.9 us
    dot_general x1, matrix products, local(): jnp.dot(encoded, encoder_first[0], preferred_element_type=jnp.float32)  10.8 us
    dot_general x1, matrix products, local(): jnp.dot(select, row_table, preferred_element_type=jnp.float32)  10.5 us
    dot_general x1, matrix products, local(): jnp.einsum('rh,rk->hk', encoded, first_delta, preferred_element_type=jnp....  10.4 us
    dot_general x1, matrix products, top_tower(): jnp.einsum('fne,hne->nfh', picked, picked, preferred_element_type=jnp.flo...  10.2 us
  transfers between devices with their start and end apart: 3, of which 3 were waited for; matrix products, arithmetic and copies ran while one was open for 4% of the time, Pallas kernels for 0%

profile of v1, /device:TPU:1, one launch (start us, length us, event | category | flops | bytes accessed | tf_op | source)
XLA Modules:
  0.0 296.4 jit_solution(6110867271017894126)
XLA Ops:
  7.2 0.0 copy-start
  7.2 0.0 copy-start.3
  7.2 0.0 copy-start.5
  7.2 10.8 %multiply_convert_fusion.2 = (bf16[768,2048]{1,0:T(8,128)(2,1)}, f32[768,2048]{1,0:T(8,128)}) fusion(bf16[1,1024,2048]{2,1,0:T(8,128)(2,1)} %param.10, s32[1,768,1024]{2,1,0:T(8,128)} %param.7), kind=kOutput, calls=%fused_computation.8 | convolution fusion | flops 3232235520 | bytes 16777216 | tf_op jit(solution)/shard_map/dot_general | solution.py:46
  18.0 0.0 copy-done.3
  18.0 0.0 copy-done.5
  18.0 10.5 %fusion.4 = bf16[8192,256]{1,0:T(8,128)(2,1)} fusion(s32[8192]{0:T(1024)S(1)} %bitcast.52, bf16[768,2048]{1,0:T(8,128)(2,1)} %get-tuple-element.3, bf16[1,2048,256]{2,1,0:T(8,128)(2,1)S(1)} %copy-done.3), kind=kOutput, calls=%fused_computation.5 | convolution fusion | flops 4035117056 | bytes 8421376 | tf_op jit(solution)/shard_map/dot_general | solution.py:58
  28.5 0.0 copy-start.1
  28.5 0.0 copy-start.2
  28.5 8.8 %all-to-all-start = ((bf16[32,256,256]{2,1,0:T(8,128)(2,1)}), bf16[32,256,256]{2,1,0:T(8,128)(2,1)}, u32[]{:S(2)}, u32[]{:S(2)}) async-start(bf16[32,256,256]{2,1,0:T(8,128)(2,1)} %bitcast.46), calls=%async_computation | async-start | bytes 8388608 | tf_op jit(solution)/shard_map/all_to_all | solution.py:62
  37.3 0.3 reduce-scatter.5.cloned.1.call-start
  37.6 0.0 copy-done.1
  37.6 0.0 copy-done.2
  37.7 49.9 %all-to-all-done = bf16[32,256,256]{2,1,0:T(8,128)(2,1)} async-done(((bf16[32,256,256]{2,1,0:T(8,128)(2,1)}), bf16[32,256,256]{2,1,0:T(8,128)(2,1)}, u32[]{:S(2)}, u32[]{:S(2)}) %all-to-all-start) | async-done | bytes 4194336 | tf_op jit(solution)/shard_map/all_to_all | solution.py:62
  87.6 10.2 %fusion.8 = f32[256,32,32]{2,1,0:T(8,128)} fusion(bf16[32,256,256]{2,1,0:T(8,128)(2,1)} %all-to-all-done), kind=kOutput, calls=%fused_computation.14 | convolution fusion | flops 134217728 | bytes 5242880 | tf_op jit(solution)/shard_map/fne,hne->nfh/dot_general | solution.py:20
  97.8 3.5 %copy.28 = f32[256,32,32]{0,2,1:T(8,128)S(1)} copy(f32[256,32,32]{2,1,0:T(8,128)} %fusion.8) | data formatting | bytes 2097152 | tf_op jit(solution)/shard_map/fne,hne->nfh/dot_general | solution.py:20
  101.3 0.1 multiply_convert_fusion.5
  101.4 0.0 copy-done
  101.4 0.7 fusion.38
  102.1 0.4 fusion.24
  102.5 1.0 fusion.20
  103.6 0.6 fusion.15
  104.2 3.7 %copy.32 = bf16[256,32,32]{2,1,0:T(8,128)(2,1)} copy(bf16[256,32,32]{0,2,1:T(8,128)(2,1)S(1)} %fusion.15) | data formatting | bytes 1048576 | tf_op jit(solution)/shard_map/convert_element_type | solution.py:34
  107.9 5.6 %fusion.5 = bf16[32,256,256]{2,0,1:T(8,128)(2,1)S(1)} fusion(bf16[256,32,32]{2,1,0:T(8,128)(2,1)} %copy.32, bf16[32,256,256]{2,1,0:T(8,128)(2,1)} %all-to-all-done), kind=kOutput, calls=%fused_computation.10 | convolution fusion | flops 138412032 | bytes 8912896 | tf_op jit(solution)/shard_map/nfh,hne->fne/dot_general | solution.py:35
  113.5 2.4 copy.33
  115.9 65.6 %all_to_all.10 = bf16[32,256,256]{2,1,0:T(8,128)(2,1)S(1)} all-to-all(bf16[32,256,256]{2,1,0:T(8,128)(2,1)S(1)} %copy.33), channel_id=1, replica_groups=mesh['feat'=32,'samp'=8] {'feat'}, dimensions={0} | all-to-all | bytes 8388608 | tf_op jit(solution)/shard_map/all_to_all | solution.py:64
  181.5 0.0 copy-start.7
  181.5 7.9 %fusion = f32[768,256]{1,0:T(8,128)S(1)} fusion(bf16[8192,256]{1,0:T(8,128)(2,1)S(1)} %bitcast.47, s32[8192]{0:T(1024)S(1)} %bitcast.53), kind=kOutput, calls=%fused_computation.1 | convolution fusion | flops 3227516928 | bytes 5013504 | tf_op jit(solution)/shard_map/nu,ne->ue/dot_general | solution.py:65
  189.3 0.0 copy-start.6
  189.3 0.9 copy-done.6
  190.2 0.0 copy-done.7
  190.2 0.0 copy-start.4
  190.2 2.1 convolution_convert_fusion.1
  192.3 0.0 reduce-scatter.5.cloned.1.call-update
  192.3 0.0 reduce-scatter.3.cloned.1.call-start
  192.4 0.0 copy-done.4
  192.4 10.4 %convolution_convert_fusion = bf16[1024,2048]{1,0:T(8,128)(2,1)} fusion(f32[768,2048]{1,0:T(8,128)} %get-tuple-element.4, bf16[1,2048,256]{2,1,0:T(8,128)(2,1)S(1)} %copy-done.4, s32[1,768,1024]{2,1,0:T(8,128)} %param.7, f32[768,256]{1,0:T(8,128)} %copy-done.6), kind=kOutput, calls=%fused_computation.13 | convolution fusion | flops 4046127104 | bytes 15466496 | tf_op jit(solution)/shard_map/rh,rk->hk/dot_general | solution.py:76
  202.8 0.0 reduce-scatter.3.cloned.1.call-update
  202.8 22.9 %reduce-scatter.5.cloned.1.call-done = bf16[256,256]{1,0:T(8,128)(2,1)} async-done(((bf16[2048,256]{1,0:T(8,128)(2,1)}), bf16[256,256]{1,0:T(8,128)(2,1)}) %reduce-scatter.5.cloned.1.call-update) | async-done | bytes 131088 | tf_op jit(solution)/shard_map/reduce_scatter | solution.py:80
  225.7 1.6 bitcast_convert_fusion.1
  227.3 60.0 %reduce-scatter.3.cloned.1.call-done = bf16[128,2048]{1,0:T(8,128)(2,1)} async-done(((bf16[1024,2048]{1,0:T(8,128)(2,1)}), bf16[128,2048]{1,0:T(8,128)(2,1)}) %reduce-scatter.3.cloned.1.call-update) | async-done | bytes 524304 | tf_op jit(solution)/shard_map/reduce_scatter | solution.py:77
  287.3 2.1 bitcast_convert_fusion
  (4 shorter events, 0.0 us)
Async XLA Ops:
  7.2 94.2 %copy-start = (bf16[1024,1024]{1,0:T(8,128)(2,1)S(1)}, bf16[1024,1024]{1,0:T(8,128)(2,1)}, u32[]{:S(2)}) copy-start(bf16[1024,1024]{1,0:T(8,128)(2,1)} %param.12) | copy-start | bytes 6291460
  7.2 10.8 %copy-start.3 = (bf16[1,2048,256]{2,1,0:T(8,128)(2,1)S(1)}, bf16[1,2048,256]{2,1,0:T(8,128)(2,1)}, u32[]{:S(2)}) copy-start(bf16[1,2048,256]{2,1,0:T(8,128)(2,1)} %param.11) | copy-start | bytes 3145732
  7.2 10.8 %copy-start.5 = (s32[1,8192]{1,0:T(1,128)S(1)}, s32[1,8192]{1,0:T(1,128)}, u32[]{:S(2)}) copy-start(s32[1,8192]{1,0:T(1,128)} %param.8) | copy-start | bytes 98308
  28.5 9.1 %copy-start.1 = (bf16[1024]{0:T(1024)(128)(2,1)S(1)}, bf16[1024]{0:T(1024)(128)(2,1)}, u32[]{:S(2)}) copy-start(bf16[1024]{0:T(1024)(128)(2,1)} %param.13) | copy-start | bytes 6148
  28.5 9.1 %copy-start.2 = (s32[256,1]{0,1:T(1,128)S(1)}, s32[256,1]{0,1:T(1,128)}, u32[]{:S(2)}) copy-start(s32[256,1]{0,1:T(1,128)} %param.9) | copy-start | bytes 3076
  28.5 59.1 %all-to-all-start = ((bf16[32,256,256]{2,1,0:T(8,128)(2,1)}), bf16[32,256,256]{2,1,0:T(8,128)(2,1)}, u32[]{:S(2)}, u32[]{:S(2)}) async-start(bf16[32,256,256]{2,1,0:T(8,128)(2,1)} %bitcast.46), calls=%async_computation | async-start | bytes 8388608 | tf_op jit(solution)/shard_map/all_to_all | solution.py:62
  37.3 188.4 %reduce-scatter.5.cloned.1.call-start = ((), (), s32[]{:S(2)}) async-start(), calls=%async_computation.5 | async-start | bytes 1179648 | tf_op jit(solution)/shard_map/reduce_scatter | solution.py:80
  181.5 8.8 %copy-start.7 = (bf16[768,2048]{1,0:T(8,128)(2,1)S(1)}, bf16[768,2048]{1,0:T(8,128)(2,1)}, u32[]{:S(2)}) copy-start(bf16[768,2048]{1,0:T(8,128)(2,1)} %get-tuple-element.3) | copy-start | bytes 9437188
  189.3 0.9 copy-start.6
  190.2 2.1 copy-start.4
  192.3 94.9 %reduce-scatter.3.cloned.1.call-start = ((), (), s32[]{:S(2)}) async-start(), calls=%async_computation.4 | async-start | bytes 4718592 | tf_op jit(solution)/shard_map/reduce_scatter | solution.py:77
Sparse Core Ops, SparseCore 0:
  192.4 33.1 reduce-scatter.4
  228.2 58.9 reduce-scatter.2

commit v2 on v1

--- a/solution.py
+++ b/solution.py
@@ -74,12 +74,20 @@
     )
     first_delta = (first_back * silu_slope(first_pre)).astype(jnp.bfloat16)
     first_local = jnp.einsum("rh,rk->hk", encoded, first_delta, preferred_element_type=jnp.float32)
-    share_first = lax.psum_scatter(
-        first_local.astype(jnp.bfloat16), "samp", scatter_dimension=0, tiled=True
-    ).astype(jnp.float32)
-    share_second = lax.psum_scatter(
-        second_local.astype(jnp.bfloat16), "samp", scatter_dimension=0, tiled=True
-    ).astype(jnp.float32)
+    group_count = lax.axis_size("samp")
+    first_rows = first_local.shape[0] // group_count
+    second_rows = second_local.shape[0] // group_count
+    hid_width = first_local.shape[1]
+    merged = jnp.concatenate(
+        [
+            first_local.astype(jnp.bfloat16).reshape(group_count, first_rows, hid_width),
+            second_local.astype(jnp.bfloat16).reshape(group_count, -1, hid_width),
+        ],
+        axis=1,
+    ).reshape(-1, hid_width)
+    share = lax.psum_scatter(merged, "samp", scatter_dimension=0, tiled=True).astype(jnp.float32)
+    share_first = share[:first_rows]
+    share_second = share[first_rows:].reshape(second_rows, emb_width)
     return (row_grads[None], share_first[None], share_second[None])
 
 

time: 300 us -> 285 us (0.950)
  waiting for transfers between devices: 133 us -> 115 us
    reduce_scatter x2 -> x1, waiting for transfers between devices: 82.8 us -> 64.8 us  [local(): lax.psum_scatter(merged, 'samp', scatter_dimension=0, tiled=True)]
    concatenate x0 -> x1, other arithmetic: none -> 5.35 us  [local(): jnp.concatenate([first_local.astype(jnp.bfloat16).reshape(group_count, fi...]
    broadcast_in_dim x2 -> x0, other arithmetic: 3.74 us -> none  [local(): return (row_grads[None], share_first[None], share_second[None])]
  transfers between devices with their start and end apart: 3 -> 2, of which waited for: 3 -> 2; matrix products, arithmetic and copies ran while one was open for 4% -> 0% of each run, Pallas kernels for 0% -> 0%
where the time goes in v2:
time: 285 us; the launch traced here: 282 us
  waiting for transfers between devices  115 us (40%)
  blocking collectives  66.1 us (23%)
  matrix products  57.6 us (20%)
  between operations  14.4 us (5%)
  local copies, waits for them, and re-layouts  12.6 us (4%)
  starting transfers between devices  9.06 us (3%)
  other arithmetic  7.29 us (3%)
    all_to_all x1, blocking collectives, local(): lax.all_to_all(emb_delta, 'feat', split_axis=0, concat_axis=0, tiled=True)  66.1 us
    reduce_scatter x1, waiting for transfers between devices, local(): lax.psum_scatter(merged, 'samp', scatter_dimension=0, tiled=True)  64.8 us
    all_to_all x1, waiting for transfers between devices, local(): lax.all_to_all(chosen_rows, 'feat', split_axis=0, concat_axis=0, tiled=True)  49.9 us
    dot_general x1, matrix products, local(): jnp.dot(encoded, encoder_first[0], preferred_element_type=jnp.float32)  10.8 us
    dot_general x1, matrix products, local(): jnp.dot(select, row_table, preferred_element_type=jnp.float32)  10.5 us
    dot_general x1, matrix products, top_tower(): jnp.einsum('fne,hne->nfh', picked, picked, preferred_element_type=jnp.flo...  10.2 us
    dot_general x1, matrix products, local(): jnp.einsum('rh,rk->hk', encoded, first_delta, preferred_element_type=jnp....  10.1 us
    all_to_all x1, starting transfers between devices, local(): lax.all_to_all(chosen_rows, 'feat', split_axis=0, concat_axis=0, tiled=True)  8.76 us
  transfers between devices with their start and end apart: 2, of which 2 were waited for; matrix products, arithmetic and copies ran while one was open for 0% of the time, Pallas kernels for 0%

profile of v2, /device:TPU:1, one launch (start us, length us, event | category | flops | bytes accessed | tf_op | source)
XLA Modules:
  0.0 281.9 jit_solution(12291744066000023239)
XLA Ops:
  7.2 0.0 copy-start
  7.2 0.0 copy-start.4
  7.2 0.0 copy-start.6
  7.2 10.8 %multiply_convert_fusion.2 = (bf16[768,2048]{1,0:T(8,128)(2,1)}, f32[768,2048]{1,0:T(8,128)}) fusion(bf16[1,1024,2048]{2,1,0:T(8,128)(2,1)} %param.10, s32[1,768,1024]{2,1,0:T(8,128)} %param.7), kind=kOutput, calls=%fused_computation.8 | convolution fusion | flops 3232235520 | bytes 16777216 | tf_op jit(solution)/shard_map/dot_general | solution.py:46
  18.0 0.0 copy-done.4
  18.0 0.0 copy-done.6
  18.0 10.5 %fusion.4 = bf16[8192,256]{1,0:T(8,128)(2,1)} fusion(s32[8192]{0:T(1024)S(1)} %bitcast.52, bf16[768,2048]{1,0:T(8,128)(2,1)} %get-tuple-element.3, bf16[1,2048,256]{2,1,0:T(8,128)(2,1)S(1)} %copy-done.4), kind=kOutput, calls=%fused_computation.5 | convolution fusion | flops 4035117056 | bytes 8421376 | tf_op jit(solution)/shard_map/dot_general | solution.py:58
  28.5 0.0 copy-start.2
  28.6 0.0 copy-start.3
  28.6 8.8 %all-to-all-start = ((bf16[32,256,256]{2,1,0:T(8,128)(2,1)}), bf16[32,256,256]{2,1,0:T(8,128)(2,1)}, u32[]{:S(2)}, u32[]{:S(2)}) async-start(bf16[32,256,256]{2,1,0:T(8,128)(2,1)} %bitcast.45), calls=%async_computation | async-start | bytes 8388608 | tf_op jit(solution)/shard_map/all_to_all | solution.py:62
  37.3 0.3 reduce-scatter.2.cloned.1.call-start
  37.6 0.0 copy-done.2
  37.7 0.0 copy-done.3
  37.7 49.9 %all-to-all-done = bf16[32,256,256]{2,1,0:T(8,128)(2,1)} async-done(((bf16[32,256,256]{2,1,0:T(8,128)(2,1)}), bf16[32,256,256]{2,1,0:T(8,128)(2,1)}, u32[]{:S(2)}, u32[]{:S(2)}) %all-to-all-start) | async-done | bytes 4194336 | tf_op jit(solution)/shard_map/all_to_all | solution.py:62
  87.6 10.2 %fusion.8 = f32[256,32,32]{2,1,0:T(8,128)} fusion(bf16[32,256,256]{2,1,0:T(8,128)(2,1)} %all-to-all-done), kind=kOutput, calls=%fused_computation.15 | convolution fusion | flops 134217728 | bytes 5242880 | tf_op jit(solution)/shard_map/fne,hne->nfh/dot_general | solution.py:20
  97.8 3.5 %copy.28 = f32[256,32,32]{0,2,1:T(8,128)S(1)} copy(f32[256,32,32]{2,1,0:T(8,128)} %fusion.8) | data formatting | bytes 2097152 | tf_op jit(solution)/shard_map/fne,hne->nfh/dot_general | solution.py:20
  101.3 0.1 multiply_convert_fusion.5
  101.4 0.0 copy-done
  101.4 0.7 fusion.38
  102.1 0.4 fusion.24
  102.6 1.0 fusion.20
  103.6 0.6 fusion.15
  104.2 3.0 %copy.32 = bf16[256,32,32]{2,1,0:T(8,128)(2,1)S(1)} copy(bf16[256,32,32]{0,2,1:T(8,128)(2,1)S(1)} %fusion.15) | data formatting | bytes 1048576 | tf_op jit(solution)/shard_map/convert_element_type | solution.py:34
  107.2 4.9 %fusion.5 = bf16[32,256,256]{2,0,1:T(8,128)(2,1)S(1)} fusion(bf16[256,32,32]{2,1,0:T(8,128)(2,1)S(1)} %copy.32, bf16[32,256,256]{2,1,0:T(8,128)(2,1)} %all-to-all-done), kind=kOutput, calls=%fused_computation.11 | convolution fusion | flops 138412032 | bytes 8912896 | tf_op jit(solution)/shard_map/nfh,hne->fne/dot_general | solution.py:35
  112.1 2.4 copy.33
  114.5 66.1 %all_to_all.10 = bf16[32,256,256]{2,1,0:T(8,128)(2,1)S(1)} all-to-all(bf16[32,256,256]{2,1,0:T(8,128)(2,1)S(1)} %copy.33), channel_id=1, replica_groups=mesh['feat'=32,'samp'=8] {'feat'}, dimensions={0} | all-to-all | bytes 8388608 | tf_op jit(solution)/shard_map/all_to_all | solution.py:64
  180.6 0.0 copy-start.8
  180.6 7.9 %fusion = f32[768,256]{1,0:T(8,128)S(1)} fusion(bf16[8192,256]{1,0:T(8,128)(2,1)S(1)} %bitcast.47, s32[8192]{0:T(1024)S(1)} %bitcast.53), kind=kOutput, calls=%fused_computation.1 | convolution fusion | flops 3227516928 | bytes 5013504 | tf_op jit(solution)/shard_map/nu,ne->ue/dot_general | solution.py:65
  188.5 0.0 copy-done.8
  188.5 0.0 copy-start.7
  188.5 0.0 copy-start.5
  188.5 1.1 convolution_convert_fusion.1
  189.6 0.0 copy-done.7
  189.6 0.4 copy-done.5
  190.0 10.1 %convolution_convert_fusion = bf16[1024,2048]{1,0:T(8,128)(2,1)} fusion(f32[768,2048]{1,0:T(8,128)} %get-tuple-element.4, bf16[1,2048,256]{2,1,0:T(8,128)(2,1)S(1)} %copy-done.5, s32[1,768,1024]{2,1,0:T(8,128)} %param.7, f32[768,256]{1,0:T(8,128)S(1)} %fusion), kind=kOutput, calls=%fused_computation.14 | convolution fusion | flops 4046127104 | bytes 15466496 | tf_op jit(solution)/shard_map/rh,rk->hk/dot_general | solution.py:76
  200.1 0.5 reshape.43
  200.6 5.3 %pad_maximum_fusion = bf16[8,160,2048]{2,1,0:T(8,128)(2,1)} fusion(bf16[8,32,2048]{2,1,0:T(8,128)(2,1)S(1)} %reshape.43, bf16[8,128,2048]{2,1,0:T(8,128)(2,1)} %bitcast.46), kind=kLoop, calls=%fused_computation.10 | loop fusion | flops 10485760 | bytes 10485760 | tf_op jit(solution)/shard_map/concatenate | solution.py:81
  206.0 0.0 copy-start.1
  206.0 0.0 reduce-scatter.2.cloned.1.call-update
  206.0 64.8 %reduce-scatter.2.cloned.1.call-done = bf16[160,2048]{1,0:T(8,128)(2,1)} async-done(((bf16[1280,2048]{1,0:T(8,128)(2,1)}), bf16[160,2048]{1,0:T(8,128)(2,1)}) %reduce-scatter.2.cloned.1.call-update) | async-done | bytes 655376 | tf_op jit(solution)/shard_map/reduce_scatter | solution.py:88
  270.9 0.9 slice.9
  271.8 0.7 broadcast_in_dim_reshape.3
  272.5 1.2 convert_element_type.83
  273.8 1.1 slice_bitcast_fusion
  274.8 0.0 copy-done.1
  (4 shorter events, 0.0 us)
Async XLA Ops:
  7.2 94.2 %copy-start = (bf16[1024,1024]{1,0:T(8,128)(2,1)S(1)}, bf16[1024,1024]{1,0:T(8,128)(2,1)}, u32[]{:S(2)}) copy-start(bf16[1024,1024]{1,0:T(8,128)(2,1)} %param.12) | copy-start | bytes 6291460
  7.2 10.8 %copy-start.4 = (bf16[1,2048,256]{2,1,0:T(8,128)(2,1)S(1)}, bf16[1,2048,256]{2,1,0:T(8,128)(2,1)}, u32[]{:S(2)}) copy-start(bf16[1,2048,256]{2,1,0:T(8,128)(2,1)} %param.11) | copy-start | bytes 3145732
  7.2 10.8 %copy-start.6 = (s32[1,8192]{1,0:T(1,128)S(1)}, s32[1,8192]{1,0:T(1,128)}, u32[]{:S(2)}) copy-start(s32[1,8192]{1,0:T(1,128)} %param.8) | copy-start | bytes 98308
  28.5 9.1 %copy-start.2 = (bf16[1024]{0:T(1024)(128)(2,1)S(1)}, bf16[1024]{0:T(1024)(128)(2,1)}, u32[]{:S(2)}) copy-start(bf16[1024]{0:T(1024)(128)(2,1)} %param.13) | copy-start | bytes 6148
  28.6 9.1 %copy-start.3 = (s32[256,1]{0,1:T(1,128)S(1)}, s32[256,1]{0,1:T(1,128)}, u32[]{:S(2)}) copy-start(s32[256,1]{0,1:T(1,128)} %param.9) | copy-start | bytes 3076
  28.6 59.0 %all-to-all-start = ((bf16[32,256,256]{2,1,0:T(8,128)(2,1)}), bf16[32,256,256]{2,1,0:T(8,128)(2,1)}, u32[]{:S(2)}, u32[]{:S(2)}) async-start(bf16[32,256,256]{2,1,0:T(8,128)(2,1)} %bitcast.45), calls=%async_computation | async-start | bytes 8388608 | tf_op jit(solution)/shard_map/all_to_all | solution.py:62
  37.3 233.5 %reduce-scatter.2.cloned.1.call-start = ((), (), s32[]{:S(2)}) async-start(), calls=%async_computation.3 | async-start | bytes 5898240 | tf_op jit(solution)/shard_map/reduce_scatter | solution.py:88
  180.6 7.9 %copy-start.8 = (bf16[768,2048]{1,0:T(8,128)(2,1)S(1)}, bf16[768,2048]{1,0:T(8,128)(2,1)}, u32[]{:S(2)}) copy-start(bf16[768,2048]{1,0:T(8,128)(2,1)} %get-tuple-element.3) | copy-start | bytes 9437188
  188.5 1.1 copy-start.7
  188.5 1.5 copy-start.5
  206.0 68.8 %copy-start.1 = (bf16[1024,1024]{1,0:T(8,128)(2,1)S(1)}, bf16[1024,1024]{1,0:T(8,128)(2,1)}, u32[]{:S(2)}) copy-start(bf16[1024,1024]{1,0:T(8,128)(2,1)} %param.12) | copy-start | bytes 6291460
Sparse Core Ops, SparseCore 0:
  206.1 64.6 reduce-scatter.1
